TPU v7x, 512 devices: a whole 4x4x16 slice. The times are simulated.
512 devices in a mesh: tile: 64 (over z, x_hi, core), chan: 8 (over x_lo, y).
Axes of the slice: x: 4 (x_hi: 2, x_lo: 2; x = x_hi * 2 + x_lo), y: 4, z: 16, core: 2. Of those that a mesh axis runs over, the one named last changes fastest.
Arguments:
- analysis: bfloat16 [64, 524288], P('chan', 'tile'), may hold values from -6 to 6
- send_rows: int32 [64, 5, 128], P('tile'), may hold values from 0 to 8191
- send_count: int32 [64, 5], P('tile'), may hold values from 64 to 128, as said below
- corner_slot: int32 [4, 2048, 256], P(None, 'tile'), may hold values from 0 to 639, as said below
- corner_weight: float32 [4, 2048, 256], P(None, 'tile'), may hold values from 0.1 to 0.6
- beside: int32 [2048, 8], P('tile'), may hold values from 0 to 2047, as said below
- quarter_turns: int32 [2048, 8], P('tile'), may hold values from 0 to 3
- kernel_one: bfloat16 [9, 128, 64], P(None, 'chan'), may hold values from -0.375 to 0.375
- kernel_two: bfloat16 [9, 128, 128], P(None, 'chan'), may hold values from -0.25 to 0.25
- kernel_three: bfloat16 [9, 128, 128], P(None, 'chan'), may hold values from -0.25 to 0.25
Outputs:
- forecast: bfloat16 [128, 2048, 256], P('chan', 'tile')
Inputs may be any that keep to these rules, and one draw needn't show every extreme that they name: send_count[s, d] is at least 64; every shard sends 128 to itself (d = 2), and some receiver gets 128 from each of its 5 senders. corner_slot[j, t, i] = d * 128 + k names a live slot, k < send_count[s, d], of the block that shard s = (e - d + 2) mod the shard count sends to the shard e holding tile t; the four corners of a pixel are slots k, k + 1, k + 2, k + 3 of one block. beside[t, k] = (t + d) mod 2048 with 1 <= |d| <= 2.
All inputs are finite; a program needn't handle non-finite values.
Results may differ from a plain program's by a relative error of at most 0.007.
Values may be sent and summed in bfloat16 or wider, within the bound.
No kernel may reach another device: no remote copies, remote signals or barrier semaphores. Data moves between devices by JAX's collectives and lax.ppermute only.
A program may use at most 64 MiB of HBM per device.

v0:
```python
import jax
import jax.numpy as jnp
import numpy as np
from jax import lax
from jax.sharding import PartitionSpec as P

P_SIZE = 16
REACH = 2


def from_behind(value, axis, steps):
    count = lax.axis_size(axis)
    pairs = [(source, (source + steps) % count) for source in range(count)]
    return lax.ppermute(value, axis, pairs)


def extended_2(x, sides, width):
    for axis, dim in sides:
        size, length = (lax.axis_size(axis), x.shape[dim])
        up = [(i, (i + 1) % size) for i in range(size)]
        down = [(j, i) for i, j in up]
        last = lax.slice_in_dim(x, length - width, length, axis=dim)
        initial = lax.slice_in_dim(x, 0, width, axis=dim)
        before = lax.ppermute(last, axis, up)
        after = lax.ppermute(initial, axis, down)
        x = jnp.concatenate([before, x, after], axis=dim)
    return x


def cycle_table(extent):
    length = 4 * extent - 4
    entries = []
    for cycle_pos in range(length):
        if cycle_pos < extent:
            row_at, col_at = (cycle_pos, 0)
        elif cycle_pos < 2 * extent - 1:
            row_at, col_at = (extent - 1, cycle_pos - extent + 1)
        elif cycle_pos < 3 * extent - 2:
            row_at, col_at = (3 * extent - 3 - cycle_pos, extent - 1)
        else:
            row_at, col_at = (0, 4 * extent - 4 - cycle_pos)
        entries.append(row_at * extent + col_at)
    return np.array(entries, np.int32)


def border_tables(extent):
    length = 4 * extent - 4
    heading = []
    anchor = []
    for col_at in range(extent):
        heading.append(0)
        anchor.append(extent - 1 + col_at)
    for col_at in range(extent):
        heading.append(1)
        anchor.append((length - col_at) % length)
    for row_at in range(extent):
        heading.append(2)
        anchor.append(3 * extent - 3 - row_at)
    for row_at in range(extent):
        heading.append(3)
        anchor.append(row_at)
    heading += [4, 5, 6, 7]
    anchor += [2 * extent - 2, extent - 1, 3 * extent - 3, 0]
    return (np.array(heading, np.int32), np.array(anchor, np.int32))


def layout_table(extent):
    padded_side = extent + 2
    interior = extent * extent
    entries = []
    for row_at in range(padded_side):
        for col_at in range(padded_side):
            if 1 <= row_at <= extent and 1 <= col_at <= extent:
                entries.append((row_at - 1) * extent + col_at - 1)
            elif row_at == 0 and 1 <= col_at <= extent:
                entries.append(interior + col_at - 1)
            elif row_at == padded_side - 1 and 1 <= col_at <= extent:
                entries.append(interior + extent + col_at - 1)
            elif col_at == 0 and 1 <= row_at <= extent:
                entries.append(interior + 2 * extent + row_at - 1)
            elif col_at == padded_side - 1 and 1 <= row_at <= extent:
                entries.append(interior + 3 * extent + row_at - 1)
            else:
                corner = (0 if row_at == 0 else 2) + (0 if col_at == 0 else 1)
                entries.append(interior + 4 * extent + corner)
    return np.array(entries, np.int32)


def conv_layer(activity, kernel, local_beside, local_turns, gather_rims):
    length = 4 * P_SIZE - 4
    cycle_vals = jnp.take(activity, cycle_table(P_SIZE), axis=2)
    extended = gather_rims(cycle_vals)
    heading, anchor = border_tables(P_SIZE)
    near_tile = jnp.take(local_beside, heading, axis=1)
    near_turn = jnp.take(local_turns, heading, axis=1)
    source = near_tile * length + jnp.remainder(anchor[None, :] - near_turn * (P_SIZE - 1), length)
    flat_cycles = extended.reshape(extended.shape[0], -1)
    border = jnp.take(flat_cycles, source.reshape(-1), axis=1)
    border = border.reshape(activity.shape[0], activity.shape[1], 4 * P_SIZE + 4)
    joined = jnp.concatenate([activity, border], axis=2)
    padded = jnp.take(joined, layout_table(P_SIZE), axis=2)
    padded_side = P_SIZE + 2
    stretch = P_SIZE * padded_side - 2
    summed = None
    for tap_index in range(9):
        offset = padded_side + 1 + (tap_index // 3 - 1) * padded_side + (tap_index % 3 - 1)
        window = padded[:, :, offset : offset + stretch]
        partial_sum = jnp.einsum(
            "oc,ctq->otq", kernel[tap_index], window, preferred_element_type=jnp.float32
        )
        summed = partial_sum if summed is None else summed + partial_sum
    summed = jnp.pad(summed, ((0, 0), (0, 0), (0, 2)))
    summed = summed.reshape(summed.shape[0], summed.shape[1], P_SIZE, padded_side)[:, :, :, :P_SIZE]
    summed = summed.reshape(summed.shape[0], summed.shape[1], P_SIZE * P_SIZE)
    return jax.nn.gelu(summed, approximate=False).astype(jnp.bfloat16)


def on_device(
    analysis,
    send_rows,
    send_count,
    corner_slot,
    corner_weight,
    beside,
    quarter_turns,
    kernel_one,
    kernel_two,
    kernel_three,
):
    shards = lax.axis_size("tile")
    groups = lax.axis_size("chan")
    tiles_here = corner_slot.shape[1]
    near_count = send_rows.shape[1]
    capacity = send_rows.shape[2]
    channels_here = analysis.shape[0]
    total_tiles = tiles_here * shards
    slot_order = jnp.arange(capacity)
    blocks = []
    for offset_index in range(near_count):
        rows_list = send_rows[0, offset_index]
        count_here = send_count[0, offset_index]
        source_block = analysis
        if offset_index != REACH:
            packed = jnp.concatenate([rows_list, count_here[None]])
            packed = from_behind(packed, "tile", offset_index - REACH)
            rows_list = packed[:capacity]
            count_here = packed[capacity]
            source_block = from_behind(analysis, "tile", offset_index - REACH)
        piece = jnp.take(source_block, rows_list, axis=1)
        piece = jnp.where(slot_order[None, :] < count_here, piece, jnp.zeros((), piece.dtype))
        blocks.append(piece)
    arrived = jnp.concatenate(blocks, axis=1)
    values = jnp.take(arrived, corner_slot.reshape(-1), axis=1)
    values = values.reshape(channels_here, 4, tiles_here, corner_slot.shape[2]).astype(jnp.float32)
    regridded = jnp.sum(values * corner_weight[None], axis=1).astype(jnp.bfloat16)
    per_group = tiles_here // groups
    activity = lax.all_to_all(regridded, "chan", split_axis=1, concat_axis=0, tiled=True)
    kernels = (
        lax.all_gather(kernel_one, "chan", axis=1, tiled=True),
        lax.all_gather(kernel_two, "chan", axis=1, tiled=True),
        lax.all_gather(kernel_three, "chan", axis=1, tiled=True),
    )
    first_tile = lax.axis_index(("tile", "chan")) * per_group
    near_beside = lax.dynamic_slice_in_dim(beside, lax.axis_index("chan") * per_group, per_group, 0)
    near_turns = lax.dynamic_slice_in_dim(
        quarter_turns, lax.axis_index("chan") * per_group, per_group, 0
    )
    local_beside = jnp.remainder(near_beside - first_tile + REACH, total_tiles)

    def joined_rims(cycle_vals):
        return extended_2(cycle_vals, ((("tile", "chan"), 1),), REACH)

    for kernel in kernels:
        activity = conv_layer(activity, kernel, local_beside, near_turns, joined_rims)
    result = lax.all_to_all(activity, "chan", split_axis=0, concat_axis=1, tiled=True)
    return result


def solution(mesh):
    return jax.shard_map(
        on_device,
        mesh=mesh,
        in_specs=(
            P("chan", "tile"),
            P("tile", None, None),
            P("tile", None),
            P(None, "tile", None),
            P(None, "tile", None),
            P("tile", None),
            P("tile", None),
            P(None, "chan", None),
            P(None, "chan", None),
            P(None, "chan", None),
        ),
        out_specs=P("chan", "tile", None),
        check_vma=False,
    )
```

profile of v0, /device:TPU:2, one launch (start us, length us, event | category | flops | bytes accessed | tf_op | source)
XLA Modules:
  0.0 374.5 jit_solution(5830040270725615998)
XLA Ops:
  0.0 13.1 %collective-permute-start.1 = (bf16[8,8192]{1,0:T(8,128)(2,1)}, bf16[8,8192]{1,0:T(8,128)(2,1)S(1)}, u32[]{:S(2)}, u32[]{:S(2)}) collective-permute-start(bf16[8,8192]{1,0:T(8,128)(2,1)} %param.32), channel_id=1, source_target_pairs={{0,496},{8,504},{16,0},{24,8},{32,16},{40,24},{48,32},{56,40},{64,... | collective-permute-start | bytes 393224 | tf_op jit(solution)/shard_map/ppermute | solution.py:14
  13.1 2.5 collective-permute-start.3
  15.6 1.9 collective-permute-start.5
  17.5 4.0 %collective-permute-start.7 = (bf16[8,8192]{1,0:T(8,128)(2,1)}, bf16[8,8192]{1,0:T(8,128)(2,1)S(1)}, u32[]{:S(2)}, u32[]{:S(2)}) collective-permute-start(bf16[8,8192]{1,0:T(8,128)(2,1)} %param.32), channel_id=1, source_target_pairs={{0,16},{8,24},{16,32},{24,40},{32,48},{40,56},{48,64},{56,72},{64,... | collective-permute-start | bytes 393224 | tf_op jit(solution)/shard_map/ppermute | solution.py:14
  21.6 1.5 fusion.74
  24.3 5.4 %collective-permute-start = (s32[129]{0:T(256)S(1)}, s32[129]{0:T(256)S(1)}, u32[]{:S(2)}, u32[]{:S(2)}) collective-permute-start(s32[129]{0:T(256)S(1)} %pad_add_fusion), channel_id=1, source_target_pairs={{0,496},{8,504},{16,0},{24,8},{32,16},{40,24},{48,32},{56,40},{64,... | collective-permute-start | bytes 1556 | tf_op jit(solution)/shard_map/ppermute | solution.py:14
  39.0 1.8 copy.262
  41.5 4.6 %collective-permute-start.2 = (s32[129]{0:T(256)S(1)}, s32[129]{0:T(256)S(1)}, u32[]{:S(2)}, u32[]{:S(2)}) collective-permute-start(s32[129]{0:T(256)S(1)} %pad_add_fusion.1), channel_id=1, source_target_pairs={{0,504},{8,0},{16,8},{24,16},{32,24},{40,32},{48,40},{56,48},{64,5... | collective-permute-start | bytes 1556 | tf_op jit(solution)/shard_map/ppermute | solution.py:14
  47.4 4.1 %collective-permute-start.4 = (s32[129]{0:T(256)S(1)}, s32[129]{0:T(256)S(1)}, u32[]{:S(2)}, u32[]{:S(2)}) collective-permute-start(s32[129]{0:T(256)S(1)} %pad_add_fusion.2), channel_id=1, source_target_pairs={{0,8},{8,16},{16,24},{24,32},{32,40},{40,48},{48,56},{56,64},{64,7... | collective-permute-start | bytes 1556 | tf_op jit(solution)/shard_map/ppermute | solution.py:14
  52.7 3.2 collective-permute-done.4
  55.9 1.9 collective-permute-start.6
  59.0 6.0 %collective-permute-done.6 = s32[129]{0:T(256)S(1)} collective-permute-done((s32[129]{0:T(256)S(1)}, s32[129]{0:T(256)S(1)}, u32[]{:S(2)}, u32[]{:S(2)}) %collective-permute-start.6) | collective-permute-done | bytes 548 | tf_op jit(solution)/shard_map/ppermute | solution.py:14
  73.7 114.2 %gather_fusion = bf16[32768,8]{1,0:T(8,128)(2,1)} fusion(bf16[8,640]{0,1:T(8,128)(2,1)S(1)} %fusion.60, s32[32768]{0:T(1024)S(1)} %broadcast_clamp_fusion), kind=kCustom, calls=%fused_computation.13 | custom fusion | bytes 1179648 | tf_op jit(solution)/shard_map/jit(_take)/gather | solution.py:153
  187.9 13.0 %multiply_reduce_fusion = bf16[8,32,256]{0,2,1:T(8,128)(2,1)S(1)} fusion(f32[4,32,256]{2,1,0:T(8,128)S(1)} %copy-done.1, bf16[8,4,32,256]{0,3,2,1:T(8,128)(2,1)} %bitcast.254, pred[4,32,256]{2,1,0:T(8,128)(4,1)S(1)} %compare_and_fusion), kind=kLoop, calls=%fused_computation.17 | loop fusion | flops 983040 | bytes 819200 | tf_op jit(solution)/shard_map/reduce_sum | solution.py:155
  202.5 5.9 %all-to-all-start = ((bf16[8,32,256]{2,0,1:T(8,128)(2,1)}), bf16[8,32,256]{2,0,1:T(8,128)(2,1)S(1)}, u32[]{:S(2)}, u32[]{:S(2)}) async-start(bf16[8,32,256]{2,0,1:T(8,128)(2,1)} %copy.266), calls=%async_computation | async-start | bytes 262144 | tf_op jit(solution)/shard_map/all_to_all | solution.py:157
  208.5 5.2 %all-to-all-done = bf16[8,32,256]{2,0,1:T(8,128)(2,1)S(1)} async-done(((bf16[8,32,256]{2,0,1:T(8,128)(2,1)}), bf16[8,32,256]{2,0,1:T(8,128)(2,1)S(1)}, u32[]{:S(2)}, u32[]{:S(2)}) %all-to-all-start) | async-done | bytes 131104 | tf_op jit(solution)/shard_map/all_to_all | solution.py:157
  214.6 2.6 collective-permute-start.8
  217.3 5.3 %collective-permute-start.9 = (bf16[64,2,60]{0,1,2:T(2,128)(2,1)S(1)}, bf16[64,2,60]{0,1,2:T(2,128)(2,1)S(1)}, u32[]{:S(2)}, u32[]{:S(2)}) collective-permute-start(bf16[64,2,60]{0,1,2:T(2,128)(2,1)S(1)} %get-tuple-element.33), channel_id=1, source_target_pairs={{1,0},{2,1},{3,2},{4,3},{5,4},{6,5},{7,6},{8,7},{9,8},{10,9},{11,1... | collective-permute-start | bytes 46088 | tf_op jit(solution)/shard_map/ppermute | solution.py:25
  222.6 29.0 %all_gather.9 = bf16[9,128,64]{2,1,0:T(8,128)(2,1)S(1)} all-gather(bf16[9,16,64]{2,1,0:T(8,128)(2,1)S(1)} %copy-done.2), channel_id=1, replica_groups=mesh['tile'=64,'chan'=8] {'chan'}, dimensions={1}, use_global_device_ids=true | all-gather | bytes 165888 | tf_op jit(solution)/shard_map/all_gather | solution.py:159
  251.9 1.4 gather_fusion.2
  253.8 2.0 gather_fusion.3
  263.0 1.9 collective-permute-start.10
  264.9 6.0 %collective-permute-start.11 = (bf16[128,2,60]{0,1,2:T(2,128)(2,1)S(1)}, bf16[128,2,60]{0,1,2:T(2,128)(2,1)S(1)}, u32[]{:S(2)}, u32[]{:S(2)}) collective-permute-start(bf16[128,2,60]{0,1,2:T(2,128)(2,1)S(1)} %get-tuple-element.31), channel_id=1, source_target_pairs={{1,0},{2,1},{3,2},{4,3},{5,4},{6,5},{7,6},{8,7},{9,8},{10,9},{11,1... | collective-permute-start | bytes 92168 | tf_op jit(solution)/shard_map/ppermute | solution.py:25
  270.9 31.7 %all_gather.10 = bf16[9,128,128]{2,1,0:T(8,128)(2,1)S(1)} all-gather(bf16[9,16,128]{2,1,0:T(8,128)(2,1)S(1)} %copy-done.3), channel_id=1, replica_groups=mesh['tile'=64,'chan'=8] {'chan'}, dimensions={1}, use_global_device_ids=true | all-gather | bytes 331776 | tf_op jit(solution)/shard_map/all_gather | solution.py:160
  302.8 1.4 gather_fusion.12
  304.8 2.0 gather_fusion.13
  312.4 2.0 collective-permute-start.12
  314.4 5.9 %collective-permute-start.13 = (bf16[128,2,60]{0,1,2:T(2,128)(2,1)S(1)}, bf16[128,2,60]{0,1,2:T(2,128)(2,1)S(1)}, u32[]{:S(2)}, u32[]{:S(2)}) collective-permute-start(bf16[128,2,60]{0,1,2:T(2,128)(2,1)S(1)} %get-tuple-element.29), channel_id=1, source_target_pairs={{1,0},{2,1},{3,2},{4,3},{5,4},{6,5},{7,6},{8,7},{9,8},{10,9},{11,1... | collective-permute-start | bytes 92168 | tf_op jit(solution)/shard_map/ppermute | solution.py:25
  320.3 31.7 %all_gather.11 = bf16[9,128,128]{2,1,0:T(8,128)(2,1)S(1)} all-gather(bf16[9,16,128]{2,1,0:T(8,128)(2,1)S(1)} %copy-done.4), channel_id=1, replica_groups=mesh['tile'=64,'chan'=8] {'chan'}, dimensions={1}, use_global_device_ids=true | all-gather | bytes 331776 | tf_op jit(solution)/shard_map/all_gather | solution.py:161
  352.3 1.4 gather_fusion.15
  354.2 2.0 gather_fusion.16
  361.1 12.5 %all_to_all.36 = bf16[128,4,256]{2,1,0:T(4,128)(2,1)S(1)} all-to-all(bf16[128,4,256]{2,1,0:T(4,128)(2,1)S(1)} %copy.324), channel_id=1, replica_groups=mesh['tile'=64,'chan'=8] {'chan'}, dimensions={0} | all-to-all | bytes 524288 | tf_op jit(solution)/shard_map/all_to_all | solution.py:175
  (173 shorter events, 46.0 us)
Async XLA Ops:
  0.0 34.5 %copy-start = (s32[32,8]{0,1:T(8,128)S(1)}, s32[32,8]{0,1:T(8,128)}, u32[]{:S(2)}) copy-start(s32[32,8]{0,1:T(8,128)} %param.38) | copy-start | bytes 3076
  0.0 66.1 %collective-permute-start.1 = (bf16[8,8192]{1,0:T(8,128)(2,1)}, bf16[8,8192]{1,0:T(8,128)(2,1)S(1)}, u32[]{:S(2)}, u32[]{:S(2)}) collective-permute-start(bf16[8,8192]{1,0:T(8,128)(2,1)} %param.32), channel_id=1, source_target_pairs={{0,496},{8,504},{16,0},{24,8},{32,16},{40,24},{48,32},{56,40},{64,... | collective-permute-start | bytes 393224 | tf_op jit(solution)/shard_map/ppermute | solution.py:14
  13.1 54.8 %collective-permute-start.3 = (bf16[8,8192]{1,0:T(8,128)(2,1)}, bf16[8,8192]{1,0:T(8,128)(2,1)S(1)}, u32[]{:S(2)}, u32[]{:S(2)}) collective-permute-start(bf16[8,8192]{1,0:T(8,128)(2,1)} %param.32), channel_id=1, source_target_pairs={{0,504},{8,0},{16,8},{24,16},{32,24},{40,32},{48,40},{56,48},{64,5... | collective-permute-start | bytes 393224 | tf_op jit(solution)/shard_map/ppermute | solution.py:14
  15.6 54.0 %collective-permute-start.5 = (bf16[8,8192]{1,0:T(8,128)(2,1)}, bf16[8,8192]{1,0:T(8,128)(2,1)S(1)}, u32[]{:S(2)}, u32[]{:S(2)}) collective-permute-start(bf16[8,8192]{1,0:T(8,128)(2,1)} %param.32), channel_id=1, source_target_pairs={{0,8},{8,16},{16,24},{24,32},{32,40},{40,48},{48,56},{56,64},{64,7... | collective-permute-start | bytes 393224 | tf_op jit(solution)/shard_map/ppermute | solution.py:14
  17.5 53.8 %collective-permute-start.7 = (bf16[8,8192]{1,0:T(8,128)(2,1)}, bf16[8,8192]{1,0:T(8,128)(2,1)S(1)}, u32[]{:S(2)}, u32[]{:S(2)}) collective-permute-start(bf16[8,8192]{1,0:T(8,128)(2,1)} %param.32), channel_id=1, source_target_pairs={{0,16},{8,24},{16,32},{24,40},{32,48},{40,56},{48,64},{56,72},{64,... | collective-permute-start | bytes 393224 | tf_op jit(solution)/shard_map/ppermute | solution.py:14
  24.3 17.2 %collective-permute-start = (s32[129]{0:T(256)S(1)}, s32[129]{0:T(256)S(1)}, u32[]{:S(2)}, u32[]{:S(2)}) collective-permute-start(s32[129]{0:T(256)S(1)} %pad_add_fusion), channel_id=1, source_target_pairs={{0,496},{8,504},{16,0},{24,8},{32,16},{40,24},{48,32},{56,40},{64,... | collective-permute-start | bytes 1556 | tf_op jit(solution)/shard_map/ppermute | solution.py:14
  41.5 5.9 %collective-permute-start.2 = (s32[129]{0:T(256)S(1)}, s32[129]{0:T(256)S(1)}, u32[]{:S(2)}, u32[]{:S(2)}) collective-permute-start(s32[129]{0:T(256)S(1)} %pad_add_fusion.1), channel_id=1, source_target_pairs={{0,504},{8,0},{16,8},{24,16},{32,24},{40,32},{48,40},{56,48},{64,5... | collective-permute-start | bytes 1556 | tf_op jit(solution)/shard_map/ppermute | solution.py:14
  47.4 8.5 %collective-permute-start.4 = (s32[129]{0:T(256)S(1)}, s32[129]{0:T(256)S(1)}, u32[]{:S(2)}, u32[]{:S(2)}) collective-permute-start(s32[129]{0:T(256)S(1)} %pad_add_fusion.2), channel_id=1, source_target_pairs={{0,8},{8,16},{16,24},{24,32},{32,40},{40,48},{48,56},{56,64},{64,7... | collective-permute-start | bytes 1556 | tf_op jit(solution)/shard_map/ppermute | solution.py:14
  55.9 9.1 %collective-permute-start.6 = (s32[129]{0:T(256)S(1)}, s32[129]{0:T(256)S(1)}, u32[]{:S(2)}, u32[]{:S(2)}) collective-permute-start(s32[129]{0:T(256)S(1)} %pad_add_fusion.3), channel_id=1, source_target_pairs={{0,16},{8,24},{16,32},{24,40},{32,48},{40,56},{48,64},{56,72},{64,... | collective-permute-start | bytes 1556 | tf_op jit(solution)/shard_map/ppermute | solution.py:14
  73.7 114.3 %copy-start.1 = (f32[4,32,256]{2,1,0:T(8,128)S(1)}, f32[4,32,256]{2,1,0:T(8,128)}, u32[]{:S(2)}) copy-start(f32[4,32,256]{2,1,0:T(8,128)} %param.36) | copy-start | bytes 393220
  200.9 7.6 %copy-start.6 = (s32[60]{0:T(128)S(1)}, s32[60]{0:T(128)}, u32[]{:S(2)}) copy-start(s32[60]{0:T(128)} %constant.232.clone) | copy-start | bytes 724
  200.9 7.6 %copy-start.5 = (s32[324]{0:T(512)S(1)}, s32[324]{0:T(512)}, u32[]{:S(2)}) copy-start(s32[324]{0:T(512)} %constant.235.clone) | copy-start | bytes 3892
  200.9 21.6 %copy-start.2 = (bf16[9,16,64]{2,1,0:T(8,128)(2,1)S(1)}, bf16[9,16,64]{2,1,0:T(8,128)(2,1)}, u32[]{:S(2)}) copy-start(bf16[9,16,64]{2,1,0:T(8,128)(2,1)} %param.39) | copy-start | bytes 55300
  202.5 11.2 %all-to-all-start = ((bf16[8,32,256]{2,0,1:T(8,128)(2,1)}), bf16[8,32,256]{2,0,1:T(8,128)(2,1)S(1)}, u32[]{:S(2)}, u32[]{:S(2)}) async-start(bf16[8,32,256]{2,0,1:T(8,128)(2,1)} %copy.266), calls=%async_computation | async-start | bytes 262144 | tf_op jit(solution)/shard_map/all_to_all | solution.py:157
  214.6 37.1 %collective-permute-start.8 = (bf16[64,2,60]{0,1,2:T(2,128)(2,1)S(1)}, bf16[64,2,60]{0,1,2:T(2,128)(2,1)S(1)}, u32[]{:S(2)}, u32[]{:S(2)}) collective-permute-start(bf16[64,2,60]{0,1,2:T(2,128)(2,1)S(1)} %get-tuple-element.32), channel_id=1, source_target_pairs={{0,1},{1,2},{2,3},{3,4},{4,5},{5,6},{6,7},{7,8},{8,9},{9,10},{10,1... | collective-permute-start | bytes 46088 | tf_op jit(solution)/shard_map/ppermute | solution.py:24
  217.3 34.5 %collective-permute-start.9 = (bf16[64,2,60]{0,1,2:T(2,128)(2,1)S(1)}, bf16[64,2,60]{0,1,2:T(2,128)(2,1)S(1)}, u32[]{:S(2)}, u32[]{:S(2)}) collective-permute-start(bf16[64,2,60]{0,1,2:T(2,128)(2,1)S(1)} %get-tuple-element.33), channel_id=1, source_target_pairs={{1,0},{2,1},{3,2},{4,3},{5,4},{6,5},{7,6},{8,7},{9,8},{10,9},{11,1... | collective-permute-start | bytes 46088 | tf_op jit(solution)/shard_map/ppermute | solution.py:25
  260.5 10.4 %copy-start.3 = (bf16[9,16,128]{2,1,0:T(8,128)(2,1)S(1)}, bf16[9,16,128]{2,1,0:T(8,128)(2,1)}, u32[]{:S(2)}) copy-start(bf16[9,16,128]{2,1,0:T(8,128)(2,1)} %param.40) | copy-start | bytes 110596
  263.0 39.7 %collective-permute-start.10 = (bf16[128,2,60]{0,1,2:T(2,128)(2,1)S(1)}, bf16[128,2,60]{0,1,2:T(2,128)(2,1)S(1)}, u32[]{:S(2)}, u32[]{:S(2)}) collective-permute-start(bf16[128,2,60]{0,1,2:T(2,128)(2,1)S(1)} %get-tuple-element.30), channel_id=1, source_target_pairs={{0,1},{1,2},{2,3},{3,4},{4,5},{5,6},{6,7},{7,8},{8,9},{9,10},{10,1... | collective-permute-start | bytes 92168 | tf_op jit(solution)/shard_map/ppermute | solution.py:24
  264.9 37.8 %collective-permute-start.11 = (bf16[128,2,60]{0,1,2:T(2,128)(2,1)S(1)}, bf16[128,2,60]{0,1,2:T(2,128)(2,1)S(1)}, u32[]{:S(2)}, u32[]{:S(2)}) collective-permute-start(bf16[128,2,60]{0,1,2:T(2,128)(2,1)S(1)} %get-tuple-element.31), channel_id=1, source_target_pairs={{1,0},{2,1},{3,2},{4,3},{5,4},{6,5},{7,6},{8,7},{9,8},{10,9},{11,1... | collective-permute-start | bytes 92168 | tf_op jit(solution)/shard_map/ppermute | solution.py:25
  309.9 10.4 %copy-start.4 = (bf16[9,16,128]{2,1,0:T(8,128)(2,1)S(1)}, bf16[9,16,128]{2,1,0:T(8,128)(2,1)}, u32[]{:S(2)}) copy-start(bf16[9,16,128]{2,1,0:T(8,128)(2,1)} %param.41) | copy-start | bytes 110596
  312.4 39.7 %collective-permute-start.12 = (bf16[128,2,60]{0,1,2:T(2,128)(2,1)S(1)}, bf16[128,2,60]{0,1,2:T(2,128)(2,1)S(1)}, u32[]{:S(2)}, u32[]{:S(2)}) collective-permute-start(bf16[128,2,60]{0,1,2:T(2,128)(2,1)S(1)} %get-tuple-element.28), channel_id=1, source_target_pairs={{0,1},{1,2},{2,3},{3,4},{4,5},{5,6},{6,7},{7,8},{8,9},{9,10},{10,1... | collective-permute-start | bytes 92168 | tf_op jit(solution)/shard_map/ppermute | solution.py:24
  314.4 37.7 %collective-permute-start.13 = (bf16[128,2,60]{0,1,2:T(2,128)(2,1)S(1)}, bf16[128,2,60]{0,1,2:T(2,128)(2,1)S(1)}, u32[]{:S(2)}, u32[]{:S(2)}) collective-permute-start(bf16[128,2,60]{0,1,2:T(2,128)(2,1)S(1)} %get-tuple-element.29), channel_id=1, source_target_pairs={{1,0},{2,1},{3,2},{4,3},{5,4},{6,5},{7,6},{8,7},{9,8},{10,9},{11,1... | collective-permute-start | bytes 92168 | tf_op jit(solution)/shard_map/ppermute | solution.py:25
where the time goes:
time: 375 us
  local copies, waits for them, and re-layouts  150 us (40%)
  blocking collectives  105 us (28%)
  starting transfers between devices  67.3 us (18%)
  other arithmetic  28.4 us (8%)
  waiting for transfers between devices  14.5 us (4%)
  matrix products  7.92 us (2%)
    gather x1, local copies, waits for them, and re-layouts, on_device(): values = jnp.take(arrived, corner_slot.reshape(-1), axis=1)  114 us
    ppermute x8, starting transfers between devices, from_behind(): return lax.ppermute(value, axis, pairs)  37.5 us
    all_gather x1, blocking collectives, on_device(): lax.all_gather(kernel_three, 'chan', axis=1, tiled=True)  31.7 us
    all_gather x1, blocking collectives, on_device(): lax.all_gather(kernel_two, 'chan', axis=1, tiled=True)  31.7 us
    all_gather x1, blocking collectives, on_device(): lax.all_gather(kernel_one, 'chan', axis=1, tiled=True)  29 us
    ppermute x3, starting transfers between devices, extended_2(): after = lax.ppermute(initial, axis, down)  17.2 us
    reduce_sum x1, other arithmetic, on_device(): jnp.sum(values * corner_weight[None], axis=1).astype(jnp.bfloat16)  13 us
    all_to_all x1, blocking collectives, on_device(): lax.all_to_all(activity, 'chan', split_axis=0, concat_axis=1, tiled=True)  12.5 us
  transfers between devices with their start and end apart: 15, of which 4 were waited for; matrix products, arithmetic and copies ran while one was open for 7% of the time, Pallas kernels for 0%

commit v1 on v0

--- a/solution.py
+++ b/solution.py
@@ -6,6 +6,13 @@
 
 P_SIZE = 16
 REACH = 2
+
+
+def shape_matrix(target, which_axis):
+    wide_out = jnp.concatenate(
+        lax.all_to_all(jnp.stack(lax.axis_size(which_axis) * [target]), which_axis, 0, 0), axis=1
+    )
+    return wide_out
 
 
 def from_behind(value, axis, steps):
@@ -157,7 +164,7 @@
     activity = lax.all_to_all(regridded, "chan", split_axis=1, concat_axis=0, tiled=True)
     kernels = (
         lax.all_gather(kernel_one, "chan", axis=1, tiled=True),
-        lax.all_gather(kernel_two, "chan", axis=1, tiled=True),
+        shape_matrix(kernel_two, "chan"),
         lax.all_gather(kernel_three, "chan", axis=1, tiled=True),
     )
     first_tile = lax.axis_index(("tile", "chan")) * per_group

time: 375 us -> 353 us (0.941)
  blocking collectives: 105 us -> 74.5 us
  starting transfers between devices: 67.3 us -> 72.5 us
    all_gather x1 -> x0, blocking collectives: 31.7 us -> none  [on_device(): lax.all_gather(kernel_two, 'chan', axis=1, tiled=True)]
    all_to_all x0 -> x1, starting transfers between devices: none -> 4.69 us  [shape_matrix(): lax.all_to_all(jnp.stack(lax.axis_size(which_axis) * [target]), which_axi...]
  transfers between devices with their start and end apart: 15 -> 16, of which waited for: 4 -> 5; matrix products, arithmetic and copies ran while one was open for 7% -> 10% of each run, Pallas kernels for 0% -> 0%
where the time goes in v1:
time: 353 us; the launch traced here: 352 us
  local copies, waits for them, and re-layouts  152 us (43%)
  blocking collectives  74.5 us (21%)
  starting transfers between devices  72.5 us (21%)
  other arithmetic  28.5 us (8%)
  waiting for transfers between devices  15.7 us (4%)
  matrix products  7.92 us (2%)
    gather x1, local copies, waits for them, and re-layouts, on_device(): values = jnp.take(arrived, corner_slot.reshape(-1), axis=1)  115 us
    ppermute x8, starting transfers between devices, from_behind(): return lax.ppermute(value, axis, pairs)  37.5 us
    all_gather x1, blocking collectives, on_device(): lax.all_gather(kernel_three, 'chan', axis=1, tiled=True)  33.1 us
    all_gather x1, blocking collectives, on_device(): lax.all_gather(kernel_one, 'chan', axis=1, tiled=True)  28.9 us
    ppermute x3, starting transfers between devices, extended_2(): after = lax.ppermute(initial, axis, down)  16.1 us
    reduce_sum x1, other arithmetic, on_device(): jnp.sum(values * corner_weight[None], axis=1).astype(jnp.bfloat16)  13 us
    all_to_all x1, blocking collectives, on_device(): lax.all_to_all(activity, 'chan', split_axis=0, concat_axis=1, tiled=True)  12.5 us
    ppermute x8, waiting for transfers between devices, from_behind(): return lax.ppermute(value, axis, pairs)  9.24 us
  transfers between devices with their start and end apart: 16, of which 5 were waited for; matrix products, arithmetic and copies ran while one was open for 10% of the time, Pallas kernels for 0%

profile of v1, /device:TPU:2, one launch (start us, length us, event | category | flops | bytes accessed | tf_op | source)
XLA Modules:
  0.0 352.3 jit_solution(8703543274926659855)
XLA Ops:
  0.0 13.1 %collective-permute-start.1 = (bf16[8,8192]{1,0:T(8,128)(2,1)}, bf16[8,8192]{1,0:T(8,128)(2,1)S(1)}, u32[]{:S(2)}, u32[]{:S(2)}) collective-permute-start(bf16[8,8192]{1,0:T(8,128)(2,1)} %param.32), channel_id=1, source_target_pairs={{0,496},{8,504},{16,0},{24,8},{32,16},{40,24},{48,32},{56,40},{64,... | collective-permute-start | bytes 393224 | tf_op jit(solution)/shard_map/ppermute | solution.py:21
  13.1 2.5 collective-permute-start.3
  15.6 1.9 collective-permute-start.5
  17.5 4.0 %collective-permute-start.7 = (bf16[8,8192]{1,0:T(8,128)(2,1)}, bf16[8,8192]{1,0:T(8,128)(2,1)S(1)}, u32[]{:S(2)}, u32[]{:S(2)}) collective-permute-start(bf16[8,8192]{1,0:T(8,128)(2,1)} %param.32), channel_id=1, source_target_pairs={{0,16},{8,24},{16,32},{24,40},{32,48},{40,56},{48,64},{56,72},{64,... | collective-permute-start | bytes 393224 | tf_op jit(solution)/shard_map/ppermute | solution.py:21
  21.6 1.5 fusion.75
  24.3 5.4 %collective-permute-start = (s32[129]{0:T(256)S(1)}, s32[129]{0:T(256)S(1)}, u32[]{:S(2)}, u32[]{:S(2)}) collective-permute-start(s32[129]{0:T(256)S(1)} %pad_add_fusion), channel_id=1, source_target_pairs={{0,496},{8,504},{16,0},{24,8},{32,16},{40,24},{48,32},{56,40},{64,... | collective-permute-start | bytes 1556 | tf_op jit(solution)/shard_map/ppermute | solution.py:21
  39.0 1.8 copy.262
  41.6 4.6 %collective-permute-start.2 = (s32[129]{0:T(256)S(1)}, s32[129]{0:T(256)S(1)}, u32[]{:S(2)}, u32[]{:S(2)}) collective-permute-start(s32[129]{0:T(256)S(1)} %pad_add_fusion.1), channel_id=1, source_target_pairs={{0,504},{8,0},{16,8},{24,16},{32,24},{40,32},{48,40},{56,48},{64,5... | collective-permute-start | bytes 1556 | tf_op jit(solution)/shard_map/ppermute | solution.py:21
  47.5 4.1 %collective-permute-start.4 = (s32[129]{0:T(256)S(1)}, s32[129]{0:T(256)S(1)}, u32[]{:S(2)}, u32[]{:S(2)}) collective-permute-start(s32[129]{0:T(256)S(1)} %pad_add_fusion.2), channel_id=1, source_target_pairs={{0,8},{8,16},{16,24},{24,32},{32,40},{40,48},{48,56},{56,64},{64,7... | collective-permute-start | bytes 1556 | tf_op jit(solution)/shard_map/ppermute | solution.py:21
  52.8 3.2 collective-permute-done.4
  55.9 1.9 collective-permute-start.6
  59.1 6.0 %collective-permute-done.6 = s32[129]{0:T(256)S(1)} collective-permute-done((s32[129]{0:T(256)S(1)}, s32[129]{0:T(256)S(1)}, u32[]{:S(2)}, u32[]{:S(2)}) %collective-permute-start.6) | collective-permute-done | bytes 548 | tf_op jit(solution)/shard_map/ppermute | solution.py:21
  73.7 115.1 %gather_fusion = bf16[32768,8]{1,0:T(8,128)(2,1)} fusion(bf16[8,640]{0,1:T(8,128)(2,1)S(1)} %fusion.60, s32[32768]{0:T(1024)S(1)} %broadcast_clamp_fusion), kind=kCustom, calls=%fused_computation.13 | custom fusion | bytes 1179648 | tf_op jit(solution)/shard_map/jit(_take)/gather | solution.py:160
  188.8 13.0 %multiply_reduce_fusion = bf16[8,32,256]{0,2,1:T(8,128)(2,1)S(1)} fusion(f32[4,32,256]{2,1,0:T(8,128)S(1)} %copy-done.1, bf16[8,4,32,256]{0,3,2,1:T(8,128)(2,1)} %bitcast.255, pred[4,32,256]{2,1,0:T(8,128)(4,1)S(1)} %compare_and_fusion), kind=kLoop, calls=%fused_computation.17 | loop fusion | flops 983040 | bytes 819200 | tf_op jit(solution)/shard_map/reduce_sum | solution.py:162
  203.5 5.9 %all-to-all-start = ((bf16[8,32,256]{2,0,1:T(8,128)(2,1)}), bf16[8,32,256]{2,0,1:T(8,128)(2,1)S(1)}, u32[]{:S(2)}, u32[]{:S(2)}) async-start(bf16[8,32,256]{2,0,1:T(8,128)(2,1)} %copy.266), calls=%async_computation | async-start | bytes 262144 | tf_op jit(solution)/shard_map/all_to_all | solution.py:164
  209.4 5.2 %all-to-all-done = bf16[8,32,256]{2,0,1:T(8,128)(2,1)S(1)} async-done(((bf16[8,32,256]{2,0,1:T(8,128)(2,1)}), bf16[8,32,256]{2,0,1:T(8,128)(2,1)S(1)}, u32[]{:S(2)}, u32[]{:S(2)}) %all-to-all-start) | async-done | bytes 131104 | tf_op jit(solution)/shard_map/all_to_all | solution.py:164
  215.4 4.7 %all-to-all-start.1 = ((bf16[8,9,16,128]{3,2,1,0:T(8,128)(2,1)}), bf16[8,9,16,128]{3,2,1,0:T(8,128)(2,1)S(1)}, u32[]{:S(2)}, u32[]{:S(2)}) async-start(bf16[8,9,16,128]{3,2,1,0:T(8,128)(2,1)} %stack.2), calls=%async_computation.1 | async-start | bytes 589824 | tf_op jit(solution)/shard_map/all_to_all | solution.py:13
  221.0 3.4 collective-permute-start.8
  224.4 4.6 %collective-permute-start.9 = (bf16[64,2,60]{0,1,2:T(2,128)(2,1)S(1)}, bf16[64,2,60]{0,1,2:T(2,128)(2,1)S(1)}, u32[]{:S(2)}, u32[]{:S(2)}) collective-permute-start(bf16[64,2,60]{0,1,2:T(2,128)(2,1)S(1)} %get-tuple-element.42), channel_id=1, source_target_pairs={{1,0},{2,1},{3,2},{4,3},{5,4},{6,5},{7,6},{8,7},{9,8},{10,9},{11,1... | collective-permute-start | bytes 46088 | tf_op jit(solution)/shard_map/ppermute | solution.py:32
  229.0 28.9 %all_gather.6 = bf16[9,128,64]{2,1,0:T(8,128)(2,1)S(1)} all-gather(bf16[9,16,64]{2,1,0:T(8,128)(2,1)S(1)} %copy-done.3), channel_id=1, replica_groups=mesh['tile'=64,'chan'=8] {'chan'}, dimensions={1}, use_global_device_ids=true | all-gather | bytes 165888 | tf_op jit(solution)/shard_map/all_gather | solution.py:166
  258.2 1.4 gather_fusion.2
  260.0 2.0 gather_fusion.3
  269.2 1.9 collective-permute-start.10
  271.1 6.3 %collective-permute-start.11 = (bf16[128,2,60]{0,1,2:T(2,128)(2,1)S(1)}, bf16[128,2,60]{0,1,2:T(2,128)(2,1)S(1)}, u32[]{:S(2)}, u32[]{:S(2)}) collective-permute-start(bf16[128,2,60]{0,1,2:T(2,128)(2,1)S(1)} %get-tuple-element.40), channel_id=1, source_target_pairs={{1,0},{2,1},{3,2},{4,3},{5,4},{6,5},{7,6},{8,7},{9,8},{10,9},{11,1... | collective-permute-start | bytes 92168 | tf_op jit(solution)/shard_map/ppermute | solution.py:32
  278.9 1.4 gather_fusion.12
  280.8 2.0 gather_fusion.13
  288.4 2.9 collective-permute-start.12
  291.4 5.3 %collective-permute-start.13 = (bf16[128,2,60]{0,1,2:T(2,128)(2,1)S(1)}, bf16[128,2,60]{0,1,2:T(2,128)(2,1)S(1)}, u32[]{:S(2)}, u32[]{:S(2)}) collective-permute-start(bf16[128,2,60]{0,1,2:T(2,128)(2,1)S(1)} %get-tuple-element.38), channel_id=1, source_target_pairs={{1,0},{2,1},{3,2},{4,3},{5,4},{6,5},{7,6},{8,7},{9,8},{10,9},{11,1... | collective-permute-start | bytes 92168 | tf_op jit(solution)/shard_map/ppermute | solution.py:32
  296.7 33.1 %all_gather.7 = bf16[9,128,128]{2,1,0:T(8,128)(2,1)S(1)} all-gather(bf16[9,16,128]{2,1,0:T(8,128)(2,1)S(1)} %copy-done.4), channel_id=1, replica_groups=mesh['tile'=64,'chan'=8] {'chan'}, dimensions={1}, use_global_device_ids=true | all-gather | bytes 331776 | tf_op jit(solution)/shard_map/all_gather | solution.py:168
  330.0 1.4 gather_fusion.15
  332.0 2.0 gather_fusion.16
  338.9 12.5 %all_to_all.41 = bf16[128,4,256]{2,1,0:T(4,128)(2,1)S(1)} all-to-all(bf16[128,4,256]{2,1,0:T(4,128)(2,1)S(1)} %copy.324), channel_id=1, replica_groups=mesh['tile'=64,'chan'=8] {'chan'}, dimensions={0} | all-to-all | bytes 524288 | tf_op jit(solution)/shard_map/all_to_all | solution.py:182
  (176 shorter events, 48.2 us)
Async XLA Ops:
  0.0 34.5 %copy-start = (s32[32,8]{0,1:T(8,128)S(1)}, s32[32,8]{0,1:T(8,128)}, u32[]{:S(2)}) copy-start(s32[32,8]{0,1:T(8,128)} %param.38) | copy-start | bytes 3076
  0.0 66.2 %collective-permute-start.1 = (bf16[8,8192]{1,0:T(8,128)(2,1)}, bf16[8,8192]{1,0:T(8,128)(2,1)S(1)}, u32[]{:S(2)}, u32[]{:S(2)}) collective-permute-start(bf16[8,8192]{1,0:T(8,128)(2,1)} %param.32), channel_id=1, source_target_pairs={{0,496},{8,504},{16,0},{24,8},{32,16},{40,24},{48,32},{56,40},{64,... | collective-permute-start | bytes 393224 | tf_op jit(solution)/shard_map/ppermute | solution.py:21
  13.1 54.9 %collective-permute-start.3 = (bf16[8,8192]{1,0:T(8,128)(2,1)}, bf16[8,8192]{1,0:T(8,128)(2,1)S(1)}, u32[]{:S(2)}, u32[]{:S(2)}) collective-permute-start(bf16[8,8192]{1,0:T(8,128)(2,1)} %param.32), channel_id=1, source_target_pairs={{0,504},{8,0},{16,8},{24,16},{32,24},{40,32},{48,40},{56,48},{64,5... | collective-permute-start | bytes 393224 | tf_op jit(solution)/shard_map/ppermute | solution.py:21
  15.6 54.1 %collective-permute-start.5 = (bf16[8,8192]{1,0:T(8,128)(2,1)}, bf16[8,8192]{1,0:T(8,128)(2,1)S(1)}, u32[]{:S(2)}, u32[]{:S(2)}) collective-permute-start(bf16[8,8192]{1,0:T(8,128)(2,1)} %param.32), channel_id=1, source_target_pairs={{0,8},{8,16},{16,24},{24,32},{32,40},{40,48},{48,56},{56,64},{64,7... | collective-permute-start | bytes 393224 | tf_op jit(solution)/shard_map/ppermute | solution.py:21
  17.5 53.9 %collective-permute-start.7 = (bf16[8,8192]{1,0:T(8,128)(2,1)}, bf16[8,8192]{1,0:T(8,128)(2,1)S(1)}, u32[]{:S(2)}, u32[]{:S(2)}) collective-permute-start(bf16[8,8192]{1,0:T(8,128)(2,1)} %param.32), channel_id=1, source_target_pairs={{0,16},{8,24},{16,32},{24,40},{32,48},{40,56},{48,64},{56,72},{64,... | collective-permute-start | bytes 393224 | tf_op jit(solution)/shard_map/ppermute | solution.py:21
  24.3 17.2 %collective-permute-start = (s32[129]{0:T(256)S(1)}, s32[129]{0:T(256)S(1)}, u32[]{:S(2)}, u32[]{:S(2)}) collective-permute-start(s32[129]{0:T(256)S(1)} %pad_add_fusion), channel_id=1, source_target_pairs={{0,496},{8,504},{16,0},{24,8},{32,16},{40,24},{48,32},{56,40},{64,... | collective-permute-start | bytes 1556 | tf_op jit(solution)/shard_map/ppermute | solution.py:21
  41.6 5.9 %collective-permute-start.2 = (s32[129]{0:T(256)S(1)}, s32[129]{0:T(256)S(1)}, u32[]{:S(2)}, u32[]{:S(2)}) collective-permute-start(s32[129]{0:T(256)S(1)} %pad_add_fusion.1), channel_id=1, source_target_pairs={{0,504},{8,0},{16,8},{24,16},{32,24},{40,32},{48,40},{56,48},{64,5... | collective-permute-start | bytes 1556 | tf_op jit(solution)/shard_map/ppermute | solution.py:21
  47.5 8.5 %collective-permute-start.4 = (s32[129]{0:T(256)S(1)}, s32[129]{0:T(256)S(1)}, u32[]{:S(2)}, u32[]{:S(2)}) collective-permute-start(s32[129]{0:T(256)S(1)} %pad_add_fusion.2), channel_id=1, source_target_pairs={{0,8},{8,16},{16,24},{24,32},{32,40},{40,48},{48,56},{56,64},{64,7... | collective-permute-start | bytes 1556 | tf_op jit(solution)/shard_map/ppermute | solution.py:21
  55.9 9.1 %collective-permute-start.6 = (s32[129]{0:T(256)S(1)}, s32[129]{0:T(256)S(1)}, u32[]{:S(2)}, u32[]{:S(2)}) collective-permute-start(s32[129]{0:T(256)S(1)} %pad_add_fusion.3), channel_id=1, source_target_pairs={{0,16},{8,24},{16,32},{24,40},{32,48},{40,56},{48,64},{56,72},{64,... | collective-permute-start | bytes 1556 | tf_op jit(solution)/shard_map/ppermute | solution.py:21
  73.7 115.1 %copy-start.1 = (f32[4,32,256]{2,1,0:T(8,128)S(1)}, f32[4,32,256]{2,1,0:T(8,128)}, u32[]{:S(2)}) copy-start(f32[4,32,256]{2,1,0:T(8,128)} %param.36) | copy-start | bytes 393220
  201.8 7.6 %copy-start.6 = (s32[60]{0:T(128)S(1)}, s32[60]{0:T(128)}, u32[]{:S(2)}) copy-start(s32[60]{0:T(128)} %constant.232.clone) | copy-start | bytes 724
  201.8 7.6 %copy-start.5 = (s32[324]{0:T(512)S(1)}, s32[324]{0:T(512)}, u32[]{:S(2)}) copy-start(s32[324]{0:T(512)} %constant.235.clone) | copy-start | bytes 3892
  201.8 12.8 %copy-start.2 = (bf16[9,16,128]{2,1,0:T(8,128)(2,1)S(1)}, bf16[9,16,128]{2,1,0:T(8,128)(2,1)}, u32[]{:S(2)}) copy-start(bf16[9,16,128]{2,1,0:T(8,128)(2,1)} %param.40) | copy-start | bytes 110596
  201.9 27.1 %copy-start.3 = (bf16[9,16,64]{2,1,0:T(8,128)(2,1)S(1)}, bf16[9,16,64]{2,1,0:T(8,128)(2,1)}, u32[]{:S(2)}) copy-start(bf16[9,16,64]{2,1,0:T(8,128)(2,1)} %param.39) | copy-start | bytes 55300
  203.5 11.2 %all-to-all-start = ((bf16[8,32,256]{2,0,1:T(8,128)(2,1)}), bf16[8,32,256]{2,0,1:T(8,128)(2,1)S(1)}, u32[]{:S(2)}, u32[]{:S(2)}) async-start(bf16[8,32,256]{2,0,1:T(8,128)(2,1)} %copy.266), calls=%async_computation | async-start | bytes 262144 | tf_op jit(solution)/shard_map/all_to_all | solution.py:164
  215.4 62.0 %all-to-all-start.1 = ((bf16[8,9,16,128]{3,2,1,0:T(8,128)(2,1)}), bf16[8,9,16,128]{3,2,1,0:T(8,128)(2,1)S(1)}, u32[]{:S(2)}, u32[]{:S(2)}) async-start(bf16[8,9,16,128]{3,2,1,0:T(8,128)(2,1)} %stack.2), calls=%async_computation.1 | async-start | bytes 589824 | tf_op jit(solution)/shard_map/all_to_all | solution.py:13
  221.0 37.0 %collective-permute-start.8 = (bf16[64,2,60]{0,1,2:T(2,128)(2,1)S(1)}, bf16[64,2,60]{0,1,2:T(2,128)(2,1)S(1)}, u32[]{:S(2)}, u32[]{:S(2)}) collective-permute-start(bf16[64,2,60]{0,1,2:T(2,128)(2,1)S(1)} %get-tuple-element.41), channel_id=1, source_target_pairs={{0,1},{1,2},{2,3},{3,4},{4,5},{5,6},{6,7},{7,8},{8,9},{9,10},{10,1... | collective-permute-start | bytes 46088 | tf_op jit(solution)/shard_map/ppermute | solution.py:31
  224.4 33.6 %collective-permute-start.9 = (bf16[64,2,60]{0,1,2:T(2,128)(2,1)S(1)}, bf16[64,2,60]{0,1,2:T(2,128)(2,1)S(1)}, u32[]{:S(2)}, u32[]{:S(2)}) collective-permute-start(bf16[64,2,60]{0,1,2:T(2,128)(2,1)S(1)} %get-tuple-element.42), channel_id=1, source_target_pairs={{1,0},{2,1},{3,2},{4,3},{5,4},{6,5},{7,6},{8,7},{9,8},{10,9},{11,1... | collective-permute-start | bytes 46088 | tf_op jit(solution)/shard_map/ppermute | solution.py:32
  269.2 8.2 %collective-permute-start.10 = (bf16[128,2,60]{0,1,2:T(2,128)(2,1)S(1)}, bf16[128,2,60]{0,1,2:T(2,128)(2,1)S(1)}, u32[]{:S(2)}, u32[]{:S(2)}) collective-permute-start(bf16[128,2,60]{0,1,2:T(2,128)(2,1)S(1)} %get-tuple-element.39), channel_id=1, source_target_pairs={{0,1},{1,2},{2,3},{3,4},{4,5},{5,6},{6,7},{7,8},{8,9},{9,10},{10,1... | collective-permute-start | bytes 92168 | tf_op jit(solution)/shard_map/ppermute | solution.py:31
  271.1 7.6 %collective-permute-start.11 = (bf16[128,2,60]{0,1,2:T(2,128)(2,1)S(1)}, bf16[128,2,60]{0,1,2:T(2,128)(2,1)S(1)}, u32[]{:S(2)}, u32[]{:S(2)}) collective-permute-start(bf16[128,2,60]{0,1,2:T(2,128)(2,1)S(1)} %get-tuple-element.40), channel_id=1, source_target_pairs={{1,0},{2,1},{3,2},{4,3},{5,4},{6,5},{7,6},{8,7},{9,8},{10,9},{11,1... | collective-permute-start | bytes 92168 | tf_op jit(solution)/shard_map/ppermute | solution.py:32
  286.0 10.7 %copy-start.4 = (bf16[9,16,128]{2,1,0:T(8,128)(2,1)S(1)}, bf16[9,16,128]{2,1,0:T(8,128)(2,1)}, u32[]{:S(2)}) copy-start(bf16[9,16,128]{2,1,0:T(8,128)(2,1)} %param.41) | copy-start | bytes 110596
  288.4 41.4 %collective-permute-start.12 = (bf16[128,2,60]{0,1,2:T(2,128)(2,1)S(1)}, bf16[128,2,60]{0,1,2:T(2,128)(2,1)S(1)}, u32[]{:S(2)}, u32[]{:S(2)}) collective-permute-start(bf16[128,2,60]{0,1,2:T(2,128)(2,1)S(1)} %get-tuple-element.37), channel_id=1, source_target_pairs={{0,1},{1,2},{2,3},{3,4},{4,5},{5,6},{6,7},{7,8},{8,9},{9,10},{10,1... | collective-permute-start | bytes 92168 | tf_op jit(solution)/shard_map/ppermute | solution.py:31
  291.4 38.5 %collective-permute-start.13 = (bf16[128,2,60]{0,1,2:T(2,128)(2,1)S(1)}, bf16[128,2,60]{0,1,2:T(2,128)(2,1)S(1)}, u32[]{:S(2)}, u32[]{:S(2)}) collective-permute-start(bf16[128,2,60]{0,1,2:T(2,128)(2,1)S(1)} %get-tuple-element.38), channel_id=1, source_target_pairs={{1,0},{2,1},{3,2},{4,3},{5,4},{6,5},{7,6},{8,7},{9,8},{10,9},{11,1... | collective-permute-start | bytes 92168 | tf_op jit(solution)/shard_map/ppermute | solution.py:32
